TPU v7x, 256 devices: a whole 4x4x8 slice. The times are simulated.
256 devices in a mesh: feat: 64 (over x, z, core), rep: 4 (over y).
Axes of the slice: x: 4, y: 4, z: 8, core: 2. Of those that a mesh axis runs over, the one named last changes fastest.
Arguments:
- features: bfloat16 [4, 128, 32768], P('rep', 'feat'), may hold values from -6 to 6
- neighbors_one: int32 [4, 15, 16384], P('rep'), may hold values from 0 to 32767, as said below
- weight_one: bfloat16 [2, 128, 256], P(None, 'feat'), may hold values from -0.375 to 0.375
- weight_two: bfloat16 [2, 256, 256], replicated, may hold values from -0.25 to 0.25
- send_rows: int32 [4, 64, 64, 32], P('rep', 'feat'), may hold values from 0 to 255
- halo_count: int32 [4, 64, 64], P('rep', 'feat'), may hold values from 1 to 32, as said below
- neighbors_two: int32 [4, 10, 16384], P('rep', None, 'feat'), may hold values from 0 to 2303, as said below
- cotangent: bfloat16 [4, 16384, 256], P('rep', 'feat'), may hold values from -6 to 6
Outputs:
- hidden_two: bfloat16 [4, 16384, 256], P('rep', 'feat')
- grad_one: float32 [2, 128, 256], P(None, 'feat')
- grad_two: float32 [2, 256, 256], replicated
Inputs may be any that keep to these rules, and one draw needn't show every extreme that they name: neighbors_one[r, k, v] lies in the block of sources from 2 * 512 * (v // 512) to 2 * 512 * (v // 512) + 2 * 512 - 1. halo_count[r, p, q] is how many halo slots shard p fills for shard q; in every replica one shard q receives exactly 32 from every shard, every other count is at most 24. send_rows[r, p, q, j] is a local row of shard p; entries with j >= halo_count[r, p, q] are ignored. `neighbors_two`: an entry below 256 is a local row; an entry 256 + p * 32 + j is a halo slot with j < halo_count[r, p, q] for the seed's shard q; every such live slot is named at least once on its shard.
All inputs are finite; a program needn't handle non-finite values.
Results may differ from a plain program's by a relative error of at most 0.0051.
Values may be sent and summed in bfloat16 or wider, within the bound.
No kernel may reach another device: no remote copies, remote signals or barrier semaphores. Data moves between devices by JAX's collectives and lax.ppermute only.
A program may use at most 64 MiB of HBM per device.

v0:
```python
import math
import jax
import jax.numpy as jnp
from jax import lax
from jax.sharding import PartitionSpec as P

BLOCK_NODES = 512


def activate(pre):
    return jnp.where(pre > 0.0, pre, jnp.expm1(jnp.minimum(pre, 0.0)))


def elu_slope(pre):
    return jnp.where(pre > 0.0, jnp.ones_like(pre), jnp.exp(jnp.minimum(pre, 0.0)))


def to_nodes(stacked):
    return lax.all_to_all(stacked, "feat", split_axis=2, concat_axis=1, tiled=True)


def block_aggregate(table_x, index_one):
    columns = table_x.shape[0]
    fanout_one = index_one.shape[0]
    layer_rows = index_one.shape[1]
    block_rows = BLOCK_NODES
    span_width = 2 * block_rows
    blocks_total = layer_rows // block_rows
    group_size = math.gcd(blocks_total, 4)
    turn_count = blocks_total // group_size
    table_parts = jnp.transpose(
        table_x.reshape(columns, turn_count, group_size, span_width), (1, 0, 2, 3)
    )
    block_base = (jnp.arange(blocks_total, dtype=jnp.int32) * span_width).reshape(
        turn_count, group_size
    )
    relative = (
        index_one.reshape(fanout_one, turn_count, group_size, block_rows)
        - block_base[None, :, :, None]
    )
    relative = jnp.transpose(relative, (1, 0, 2, 3))

    def one_turn(pair):
        table_part, relative_part = pair
        positions = lax.broadcasted_iota(jnp.int32, (group_size, block_rows, span_width), 2)
        tallies = jnp.zeros((group_size, block_rows, span_width), jnp.bfloat16)
        for sample in range(fanout_one):
            tallies = tallies + (relative_part[sample][:, :, None] == positions).astype(
                jnp.bfloat16
            )
        summed = jnp.einsum("cgs,gvs->cgv", table_part, tallies, preferred_element_type=jnp.float32)
        return (summed / fanout_one).astype(jnp.bfloat16)

    gathered = lax.map(one_turn, (table_parts, relative))
    return jnp.transpose(gathered, (1, 0, 2, 3)).reshape(columns, layer_rows)


def on_device(
    features, neighbors_one, weight_one, weight_two, send_rows, halo_count, neighbors_two, cotangent
):
    feat_devs = lax.axis_size("feat")
    rep_devs = lax.axis_size("rep")
    table_x = features[0]
    index_one = neighbors_one[0]
    layer_rows = index_one.shape[1]
    node_count = layer_rows // feat_devs
    hidden_width = weight_one.shape[2]
    aggregate_one = block_aggregate(table_x, index_one)
    stacked = jnp.stack([table_x[:, :layer_rows], aggregate_one])
    node_feats = None
    node_feats = to_nodes(stacked)
    full_weight = lax.all_gather(weight_one, "feat", axis=1, tiled=True)
    pre_one = jnp.einsum("sfr,sfh->rh", node_feats, full_weight, preferred_element_type=jnp.float32)
    hidden_one = activate(pre_one).astype(jnp.bfloat16)
    send_slots = send_rows[0, 0]
    counts = halo_count[0, 0]
    capacity = send_slots.shape[1]
    live_slots = lax.broadcasted_iota(jnp.int32, send_slots.shape, 1) < counts[:, None]
    outgoing = jnp.where(
        live_slots[:, :, None], hidden_one[send_slots], jnp.zeros((), jnp.bfloat16)
    )
    incoming = lax.all_to_all(outgoing, "feat", split_axis=0, concat_axis=0, tiled=True)
    table_two = jnp.concatenate(
        [hidden_one, incoming.reshape(feat_devs * capacity, hidden_width)], axis=0
    )
    index_two = neighbors_two[0]
    fanout_two = index_two.shape[0]
    seed_rows = index_two.shape[1]
    summed_two = jnp.zeros((seed_rows, hidden_width), jnp.float32)
    for sample in range(fanout_two):
        summed_two = summed_two + table_two[index_two[sample]].astype(jnp.float32)
    aggregate_two = (summed_two / fanout_two).astype(jnp.bfloat16)
    pre_two = jnp.dot(hidden_one, weight_two[0], preferred_element_type=jnp.float32) + jnp.dot(
        aggregate_two, weight_two[1], preferred_element_type=jnp.float32
    )
    hidden_two = activate(pre_two).astype(jnp.bfloat16)
    grad_scale = 1.0 / math.sqrt(rep_devs * feat_devs * seed_rows)
    slope_two = (cotangent[0].astype(jnp.float32) * elu_slope(pre_two) * grad_scale).astype(
        jnp.bfloat16
    )
    local_two = jnp.stack(
        [
            jnp.einsum("rh,rk->hk", hidden_one, slope_two, preferred_element_type=jnp.float32),
            jnp.einsum("rh,rk->hk", aggregate_two, slope_two, preferred_element_type=jnp.float32),
        ]
    )
    grad_two = lax.psum(local_two, ("feat", "rep"))
    back_self = jnp.einsum(
        "rk,hk->rh", slope_two, weight_two[0], preferred_element_type=jnp.float32
    )
    back_agg = (
        jnp.einsum("rk,hk->rh", slope_two, weight_two[1], preferred_element_type=jnp.float32)
        / fanout_two
    )
    grad_table = jnp.zeros((table_two.shape[0], hidden_width), jnp.float32)
    for sample in range(fanout_two):
        grad_table = grad_table.at[index_two[sample]].add(back_agg)
    grad_table = grad_table.at[:seed_rows].add(back_self)
    returned = lax.all_to_all(
        grad_table[node_count:].reshape(feat_devs, capacity, hidden_width).astype(jnp.bfloat16),
        "feat",
        split_axis=0,
        concat_axis=0,
        tiled=True,
    ).astype(jnp.float32)
    returned = jnp.where(live_slots[:, :, None], returned, 0.0)
    back_one = grad_table[:node_count].at[send_slots].add(returned)
    slope_one = (back_one * elu_slope(pre_one)).astype(jnp.bfloat16)
    first_local = jnp.einsum(
        "scr,rh->sch",
        stacked,
        lax.all_gather(slope_one, "feat", axis=0, tiled=True),
        preferred_element_type=jnp.float32,
    )
    grad_one = lax.psum(first_local, "rep")
    return (hidden_two[None], grad_one, grad_two)


def solution(mesh):
    return jax.shard_map(
        on_device,
        mesh=mesh,
        in_specs=(
            P("rep", "feat", None),
            P("rep", None, None),
            P(None, "feat", None),
            P(),
            P("rep", "feat", None, None),
            P("rep", "feat", None),
            P("rep", None, "feat"),
            P("rep", "feat", None),
        ),
        out_specs=(P("rep", "feat", None), P(None, "feat", None), P()),
        check_vma=False,
    )
```

profile of v0, /device:TPU:2, one launch (start us, length us, event | category | flops | bytes accessed | tf_op | source)
XLA Modules:
  0.0 702.0 jit_solution(11061386898485496683)
XLA Ops:
  8.0 3.6 reduce.2
  12.6 151.7 %while.11 = (s32[]{:T(128)}, bf16[8,2,4,512]{3,1,2,0:T(2,128)(2,1)S(1)}, s32[8,15,4,512]{3,2,0,1:T(4,128)S(1)}, bf16[8,2,4,1024]{3,1,2,0:T(2,128)(2,1)S(1)}, s32[]{:T(128)}) while((s32[]{:T(128)}, bf16[8,2,4,512]{3,1,2,0:T(2,128)(2,1)S(1)}, s32[8,15,4,512]{3,2,0,1:T(4,128)S(1)}, bf16[8,2,4,1024]{3,1,2,0:T(2,128)(2,1)S(1)}, s32[]{:T(128)}) %tuple.63), condition=%wide.region_1.2_spmd, body=%wide.region_0.1_spmd.sunk | while | flops 134225920 | bytes 671825 | solution.py:54
  12.7 18.9 %fusion.123 = bf16[8,2,4,512]{3,1,2,0:T(2,128)(2,1)S(1)} fusion(bf16[8,2,4,512]{3,1,2,0:T(2,128)(2,1)S(1)} %get-tuple-element.144, s32[]{:T(128)S(6)} %copy.35, s32[4,512]{1,0:T(4,128)S(1)} %get-tuple-element.123, s32[4,512]{1,0:T(4,128)S(1)} %get-tuple-element.124, s32[4,512]{1,0:T(4,128)S(1)} %get-tuple-element.125, ...), kind=kOutput, calls=%fused_computation.85.clone.3 | convolution fusion | flops 134225920 | bytes 147460 | tf_op jit(solution)/shard_map/while/body/eval_jaxpr/cgs,gvs->cgv/dot_general | solution.py:51
  31.6 18.9 %fusion.123 = bf16[8,2,4,512]{3,1,2,0:T(2,128)(2,1)S(1)} fusion(bf16[8,2,4,512]{3,1,2,0:T(2,128)(2,1)S(1)} %get-tuple-element.144, s32[]{:T(128)S(6)} %copy.35, s32[4,512]{1,0:T(4,128)S(1)} %get-tuple-element.123, s32[4,512]{1,0:T(4,128)S(1)} %get-tuple-element.124, s32[4,512]{1,0:T(4,128)S(1)} %get-tuple-element.125, ...), kind=kOutput, calls=%fused_computation.85.clone.3 | convolution fusion | flops 134225920 | bytes 147460 | tf_op jit(solution)/shard_map/while/body/eval_jaxpr/cgs,gvs->cgv/dot_general | solution.py:51
  50.6 18.9 %fusion.123 = bf16[8,2,4,512]{3,1,2,0:T(2,128)(2,1)S(1)} fusion(bf16[8,2,4,512]{3,1,2,0:T(2,128)(2,1)S(1)} %get-tuple-element.144, s32[]{:T(128)S(6)} %copy.35, s32[4,512]{1,0:T(4,128)S(1)} %get-tuple-element.123, s32[4,512]{1,0:T(4,128)S(1)} %get-tuple-element.124, s32[4,512]{1,0:T(4,128)S(1)} %get-tuple-element.125, ...), kind=kOutput, calls=%fused_computation.85.clone.3 | convolution fusion | flops 134225920 | bytes 147460 | tf_op jit(solution)/shard_map/while/body/eval_jaxpr/cgs,gvs->cgv/dot_general | solution.py:51
  69.5 18.9 %fusion.123 = bf16[8,2,4,512]{3,1,2,0:T(2,128)(2,1)S(1)} fusion(bf16[8,2,4,512]{3,1,2,0:T(2,128)(2,1)S(1)} %get-tuple-element.144, s32[]{:T(128)S(6)} %copy.35, s32[4,512]{1,0:T(4,128)S(1)} %get-tuple-element.123, s32[4,512]{1,0:T(4,128)S(1)} %get-tuple-element.124, s32[4,512]{1,0:T(4,128)S(1)} %get-tuple-element.125, ...), kind=kOutput, calls=%fused_computation.85.clone.3 | convolution fusion | flops 134225920 | bytes 147460 | tf_op jit(solution)/shard_map/while/body/eval_jaxpr/cgs,gvs->cgv/dot_general | solution.py:51
  88.5 18.9 %fusion.123 = bf16[8,2,4,512]{3,1,2,0:T(2,128)(2,1)S(1)} fusion(bf16[8,2,4,512]{3,1,2,0:T(2,128)(2,1)S(1)} %get-tuple-element.144, s32[]{:T(128)S(6)} %copy.35, s32[4,512]{1,0:T(4,128)S(1)} %get-tuple-element.123, s32[4,512]{1,0:T(4,128)S(1)} %get-tuple-element.124, s32[4,512]{1,0:T(4,128)S(1)} %get-tuple-element.125, ...), kind=kOutput, calls=%fused_computation.85.clone.3 | convolution fusion | flops 134225920 | bytes 147460 | tf_op jit(solution)/shard_map/while/body/eval_jaxpr/cgs,gvs->cgv/dot_general | solution.py:51
  107.5 18.9 %fusion.123 = bf16[8,2,4,512]{3,1,2,0:T(2,128)(2,1)S(1)} fusion(bf16[8,2,4,512]{3,1,2,0:T(2,128)(2,1)S(1)} %get-tuple-element.144, s32[]{:T(128)S(6)} %copy.35, s32[4,512]{1,0:T(4,128)S(1)} %get-tuple-element.123, s32[4,512]{1,0:T(4,128)S(1)} %get-tuple-element.124, s32[4,512]{1,0:T(4,128)S(1)} %get-tuple-element.125, ...), kind=kOutput, calls=%fused_computation.85.clone.3 | convolution fusion | flops 134225920 | bytes 147460 | tf_op jit(solution)/shard_map/while/body/eval_jaxpr/cgs,gvs->cgv/dot_general | solution.py:51
  126.4 18.9 %fusion.123 = bf16[8,2,4,512]{3,1,2,0:T(2,128)(2,1)S(1)} fusion(bf16[8,2,4,512]{3,1,2,0:T(2,128)(2,1)S(1)} %get-tuple-element.144, s32[]{:T(128)S(6)} %copy.35, s32[4,512]{1,0:T(4,128)S(1)} %get-tuple-element.123, s32[4,512]{1,0:T(4,128)S(1)} %get-tuple-element.124, s32[4,512]{1,0:T(4,128)S(1)} %get-tuple-element.125, ...), kind=kOutput, calls=%fused_computation.85.clone.3 | convolution fusion | flops 134225920 | bytes 147460 | tf_op jit(solution)/shard_map/while/body/eval_jaxpr/cgs,gvs->cgv/dot_general | solution.py:51
  145.4 18.9 %fusion.123 = bf16[8,2,4,512]{3,1,2,0:T(2,128)(2,1)S(1)} fusion(bf16[8,2,4,512]{3,1,2,0:T(2,128)(2,1)S(1)} %get-tuple-element.144, s32[]{:T(128)S(6)} %copy.35, s32[4,512]{1,0:T(4,128)S(1)} %get-tuple-element.123, s32[4,512]{1,0:T(4,128)S(1)} %get-tuple-element.124, s32[4,512]{1,0:T(4,128)S(1)} %get-tuple-element.125, ...), kind=kOutput, calls=%fused_computation.85.clone.3 | convolution fusion | flops 134225920 | bytes 147460 | tf_op jit(solution)/shard_map/while/body/eval_jaxpr/cgs,gvs->cgv/dot_general | solution.py:51
  164.5 12.9 %copy.17 = bf16[2,2,16384]{1,0,2:T(2,128)(2,1)} copy(bf16[2,2,16384]{2,1,0:T(2,128)(2,1)S(1)} %pad_maximum_fusion.2) | data formatting | bytes 262144 | tf_op jit(solution)/shard_map/stack | solution.py:69
  177.5 13.7 %reshape.627 = bf16[64,2,512]{2,1,0:T(2,128)(2,1)} reshape(bf16[16384,2,2]{2,1,0:T(2,128)(2,1)} %bitcast.148) | data formatting | bytes 262144
  191.2 12.0 %all-to-all-start = ((bf16[64,2,512]{2,1,0:T(2,128)(2,1)}), bf16[64,2,512]{2,1,0:T(2,128)(2,1)S(1)}, u32[]{:S(2)}, u32[]{:S(2)}) async-start(bf16[64,2,512]{2,1,0:T(2,128)(2,1)} %reshape.627), calls=%async_computation | async-start | bytes 262144 | tf_op jit(solution)/shard_map/all_to_all | solution.py:19
  203.5 49.5 %all_gather.6 = bf16[2,128,256]{2,0,1:T(2,128)(2,1)S(1)} all-gather(bf16[2,2,256]{2,0,1:T(2,128)(2,1)S(1)} %copy.19), channel_id=1, replica_groups=mesh['feat'=64,'rep'=4] {'feat'}, dimensions={1}, use_global_device_ids=true | all-gather | bytes 133120 | tf_op jit(solution)/shard_map/all_gather | solution.py:72
  253.0 19.1 %reshape.628 = bf16[16384,2,2]{2,1,0:T(2,128)(2,1)} reshape(bf16[64,2,512]{2,1,0:T(2,128)(2,1)S(1)} %all-to-all-done) | data formatting | bytes 262144
  272.0 16.5 %copy.18 = bf16[2,2,64,256]{3,0,1,2:T(2,128)(2,1)S(1)} copy(bf16[2,2,64,256]{1,0,3,2:T(2,128)(2,1)} %bitcast.149) | data formatting | bytes 262144 | tf_op jit(solution)/shard_map/all_to_all | solution.py:19
  289.5 7.5 %gather_fusion = bf16[2048,256]{1,0:T(8,128)(2,1)S(1)} fusion(bf16[256,256]{1,0:T(8,128)(2,1)S(1)} %get-tuple-element.81, s32[2048]{0:T(1024)S(1)} %broadcast_clamp_fusion), kind=kCustom, calls=%fused_computation | custom fusion | bytes 2105344 | tf_op jit(solution)/shard_map/gather | solution.py:80
  298.3 9.2 %all-to-all-start.1 = ((bf16[64,32,256]{2,1,0:T(8,128)(2,1)}), bf16[64,32,256]{2,1,0:T(8,128)(2,1)S(1)}, u32[]{:S(2)}, u32[]{:S(2)}) async-start(bf16[64,32,256]{2,1,0:T(8,128)(2,1)} %broadcast_select_fusion), calls=%async_computation.1 | async-start | bytes 2097152 | tf_op jit(solution)/shard_map/all_to_all | solution.py:82
  307.9 26.5 %all-to-all-done.1 = bf16[64,32,256]{2,1,0:T(8,128)(2,1)S(1)} async-done(((bf16[64,32,256]{2,1,0:T(8,128)(2,1)}), bf16[64,32,256]{2,1,0:T(8,128)(2,1)S(1)}, u32[]{:S(2)}, u32[]{:S(2)}) %all-to-all-start.1) | async-done | bytes 1048608 | tf_op jit(solution)/shard_map/all_to_all | solution.py:82
  350.7 2.8 scatter_fusion
  353.5 2.8 scatter_fusion.1
  356.4 3.0 scatter_fusion.2
  359.4 2.8 scatter_fusion.3
  362.2 2.8 scatter_fusion.4
  365.0 2.8 scatter_fusion.5
  377.5 8.0 %all-to-all-start.2 = ((bf16[64,32,256]{2,1,0:T(8,128)(2,1)}), bf16[64,32,256]{2,1,0:T(8,128)(2,1)}, u32[]{:S(2)}, u32[]{:S(2)}) async-start(bf16[64,32,256]{2,1,0:T(8,128)(2,1)} %bitcast.57), calls=%async_computation.2 | async-start | bytes 2097152 | tf_op jit(solution)/shard_map/all_to_all | solution.py:119
  385.7 26.6 %all-to-all-done.2 = bf16[64,32,256]{2,1,0:T(8,128)(2,1)} async-done(((bf16[64,32,256]{2,1,0:T(8,128)(2,1)}), bf16[64,32,256]{2,1,0:T(8,128)(2,1)}, u32[]{:S(2)}, u32[]{:S(2)}) %all-to-all-start.2) | async-done | bytes 1048608 | tf_op jit(solution)/shard_map/all_to_all | solution.py:119
  413.9 11.9 %scatter_fusion.9 = f32[256,256]{1,0:T(8,128)S(1)} fusion(f32[256,256]{1,0:T(8,128)S(1)} %convolution_add_fusion, s32[2048]{0:T(1024)S(1)} %reshape.446, f32[2048,256]{1,0:T(8,128)S(1)} %bitcast.150), kind=kCustom, calls=%fused_computation.21 | custom fusion | flops 524288 | bytes 6299648 | tf_op jit(solution)/shard_map/scatter-add | solution.py:127
  427.9 79.4 %all-gather.2.cloned.1.call-done = bf16[16384,256]{1,0:T(8,128)(2,1)} async-done(((bf16[256,256]{1,0:T(8,128)(2,1)}), bf16[16384,256]{1,0:T(8,128)(2,1)}) %all-gather.2.cloned.1.call-update) | async-done | bytes 8388624 | tf_op jit(solution)/shard_map/all_gather | solution.py:132
  507.3 4.7 fusion.75
  512.0 11.0 %psum.14 = f32[2,2,256]{2,1,0:T(2,128)} all-reduce(f32[2,2,256]{2,1,0:T(2,128)S(1)} %fusion.75), channel_id=1, replica_groups=mesh['feat'=64,'rep'=4] {'rep'}, use_global_device_ids=true, to_apply=%region_13.14 | all-reduce | flops 1024 | bytes 8192 | tf_op jit(solution)/shard_map/psum | solution.py:135
  523.0 169.4 %all-reduce.2.cloned.1.call-done = f32[2,256,256]{2,1,0:T(8,128)} async-done(((f32[2,256,256]{2,1,0:T(8,128)}), f32[2,256,256]{2,1,0:T(8,128)}) %all-reduce.2.cloned.1.call-update) | async-done | bytes 524304 | tf_op jit(solution)/shard_map/psum | solution.py:107
  (95 shorter events, 36.0 us)
Async XLA Ops:
  8.0 4.6 copy-start.2
  177.4 25.8 %copy-start.3 = (s32[1,1,64,32]{2,3,1,0:T(8,128)S(1)}, s32[1,1,64,32]{2,3,1,0:T(8,128)}, u32[]{:S(2)}) copy-start(s32[1,1,64,32]{2,3,1,0:T(8,128)} %param.16) | copy-start | bytes 24580
  177.4 25.8 %copy-start.6 = (s32[1,1,64]{2,1,0:T(1,128)S(1)}, s32[1,1,64]{2,1,0:T(1,128)}, u32[]{:S(2)}) copy-start(s32[1,1,64]{2,1,0:T(1,128)} %param.17) | copy-start | bytes 772
  177.5 25.9 %copy-start.5 = (bf16[2,2,256]{2,1,0:T(2,128)(2,1)S(1)}, bf16[2,2,256]{2,1,0:T(2,128)(2,1)}, u32[]{:S(2)}) copy-start(bf16[2,2,256]{2,1,0:T(2,128)(2,1)} %param.14) | copy-start | bytes 6148
  191.2 61.8 %all-to-all-start = ((bf16[64,2,512]{2,1,0:T(2,128)(2,1)}), bf16[64,2,512]{2,1,0:T(2,128)(2,1)S(1)}, u32[]{:S(2)}, u32[]{:S(2)}) async-start(bf16[64,2,512]{2,1,0:T(2,128)(2,1)} %reshape.627), calls=%async_computation | async-start | bytes 262144 | tf_op jit(solution)/shard_map/all_to_all | solution.py:19
  297.0 10.5 %copy-start.4 = (s32[1,10,256]{2,0,1:T(1,128)S(1)}, s32[1,10,256]{2,0,1:T(1,128)}, u32[]{:S(2)}) copy-start(s32[1,10,256]{2,0,1:T(1,128)} %param.18) | copy-start | bytes 30724
  297.0 10.7 %copy-start = (bf16[2,256,256]{2,1,0:T(8,128)(2,1)S(1)}, bf16[2,256,256]{2,1,0:T(8,128)(2,1)}, u32[]{:S(2)}) copy-start(bf16[2,256,256]{2,1,0:T(8,128)(2,1)} %param.15) | copy-start | bytes 786436
  298.3 36.0 %all-to-all-start.1 = ((bf16[64,32,256]{2,1,0:T(8,128)(2,1)}), bf16[64,32,256]{2,1,0:T(8,128)(2,1)S(1)}, u32[]{:S(2)}, u32[]{:S(2)}) async-start(bf16[64,32,256]{2,1,0:T(8,128)(2,1)} %broadcast_select_fusion), calls=%async_computation.1 | async-start | bytes 2097152 | tf_op jit(solution)/shard_map/all_to_all | solution.py:82
  377.5 34.8 %all-to-all-start.2 = ((bf16[64,32,256]{2,1,0:T(8,128)(2,1)}), bf16[64,32,256]{2,1,0:T(8,128)(2,1)}, u32[]{:S(2)}, u32[]{:S(2)}) async-start(bf16[64,32,256]{2,1,0:T(8,128)(2,1)} %bitcast.57), calls=%async_computation.2 | async-start | bytes 2097152 | tf_op jit(solution)/shard_map/all_to_all | solution.py:119
  385.5 121.8 %all-gather.2.cloned.1.call-start = ((), (), s32[]{:S(2)}) async-start(), calls=%async_computation.3 | async-start | bytes 8519680 | tf_op jit(solution)/shard_map/all_gather | solution.py:132
  413.9 11.9 %copy-start.1 = (f32[256,256]{1,0:T(8,128)S(1)}, f32[256,256]{1,0:T(8,128)}, u32[]{:S(2)}) copy-start(f32[256,256]{1,0:T(8,128)} %get-tuple-element.82) | copy-start | bytes 786436
  426.6 265.9 %all-reduce.2.cloned.1.call-start = ((), (), s32[]{:S(2)}) async-start(), calls=%async_computation.4 | async-start | bytes 1048576 | tf_op jit(solution)/shard_map/psum | solution.py:107
Sparse Core Ops, SparseCore 0:
  426.7 80.5 all-gather.1
Sparse Core Ops, SparseCore 1:
  433.1 259.3 all-reduce.1
where the time goes:
time: 711 us; the launch traced here: 702 us
  waiting for transfers between devices  302 us (42%)
  matrix products  160 us (23%)
  local copies, waits for them, and re-layouts  85.5 us (12%)
  blocking collectives  60.5 us (9%)
  other arithmetic  48.8 us (7%)
  starting transfers between devices  29.3 us (4%)
  between operations  16.1 us (2%)
    psum x1, waiting for transfers between devices, on_device(): grad_two = lax.psum(local_two, ('feat', 'rep'))  169 us
    dot_general x8, matrix products, one_turn(): jnp.einsum('cgs,gvs->cgv', table_part, tallies, preferred_element_type=jn...  151 us
    all_gather x1, waiting for transfers between devices, on_device(): lax.all_gather(slope_one, 'feat', axis=0, tiled=True)  79.4 us
    all_gather x1, blocking collectives, on_device(): full_weight = lax.all_gather(weight_one, 'feat', axis=1, tiled=True)  49.5 us
    unnamed x18, local copies, waits for them, and re-layouts  34.7 us
    scatter-add x10, other arithmetic, on_device(): grad_table = grad_table.at[index_two[sample]].add(back_agg)  28.1 us
    all_to_all x1, waiting for transfers between devices, on_device(): lax.all_to_all(grad_table[node_count:].reshape(feat_devs, capacity, hidde...  26.6 us
    all_to_all x1, waiting for transfers between devices, on_device(): lax.all_to_all(outgoing, 'feat', split_axis=0, concat_axis=0, tiled=True)  26.5 us
  transfers between devices with their start and end apart: 5, of which 4 were waited for; matrix products, arithmetic and copies ran while one was open for 1% of the time, Pallas kernels for 0%

commit v1 on v0

--- a/solution.py
+++ b/solution.py
@@ -69,7 +69,9 @@
     stacked = jnp.stack([table_x[:, :layer_rows], aggregate_one])
     node_feats = None
     node_feats = to_nodes(stacked)
-    full_weight = lax.all_gather(weight_one, "feat", axis=1, tiled=True)
+    full_weight = jnp.concatenate(
+        lax.all_to_all(jnp.stack([weight_one] * lax.axis_size("feat")), "feat", 0, 0), axis=1
+    )
     pre_one = jnp.einsum("sfr,sfh->rh", node_feats, full_weight, preferred_element_type=jnp.float32)
     hidden_one = activate(pre_one).astype(jnp.bfloat16)
     send_slots = send_rows[0, 0]

time: 711 us -> 679 us (0.955)
  blocking collectives: 60.5 us -> 11.1 us
  waiting for transfers between devices: 302 us -> 310 us
    all_gather x1 -> x0, blocking collectives: 49.5 us -> none  [on_device(): full_weight = lax.all_gather(weight_one, 'feat', axis=1, tiled=True)]
    all_to_all x0 -> x1, starting transfers between devices: none -> 12 us  [on_device(): lax.all_to_all(jnp.stack([weight_one] * lax.axis_size('feat')), 'feat', 0...]
    all_to_all x1, waiting for transfers between devices: 0.01 us -> 8.95 us  [to_nodes(): lax.all_to_all(stacked, 'feat', split_axis=2, concat_axis=1, tiled=True)]
    unnamed x18 -> x15, local copies, waits for them, and re-layouts: 34.7 us -> 34.6 us
  transfers between devices with their start and end apart: 5 -> 6, of which waited for: 4 -> 5; matrix products, arithmetic and copies ran while one was open for 1% -> 28% of each run, Pallas kernels for 0% -> 0%
where the time goes in v1:
time: 679 us; the launch traced here: 670 us
  waiting for transfers between devices  310 us (46%)
  matrix products  160 us (24%)
  local copies, waits for them, and re-layouts  87.1 us (13%)
  other arithmetic  48.8 us (7%)
  starting transfers between devices  36.4 us (5%)
  between operations  16.1 us (2%)
  blocking collectives  11.1 us (2%)
    psum x1, waiting for transfers between devices, on_device(): grad_two = lax.psum(local_two, ('feat', 'rep'))  169 us
    dot_general x8, matrix products, one_turn(): jnp.einsum('cgs,gvs->cgv', table_part, tallies, preferred_element_type=jn...  151 us
    all_gather x1, waiting for transfers between devices, on_device(): lax.all_gather(slope_one, 'feat', axis=0, tiled=True)  79.4 us
    unnamed x15, local copies, waits for them, and re-layouts  34.6 us
    scatter-add x10, other arithmetic, on_device(): grad_table = grad_table.at[index_two[sample]].add(back_agg)  28.1 us
    all_to_all x1, waiting for transfers between devices, on_device(): lax.all_to_all(outgoing, 'feat', split_axis=0, concat_axis=0, tiled=True)  26.6 us
    all_to_all x1, waiting for transfers between devices, on_device(): lax.all_to_all(grad_table[node_count:].reshape(feat_devs, capacity, hidde...  26.6 us
    all_to_all x1, local copies, waits for them, and re-layouts, to_nodes(): lax.all_to_all(stacked, 'feat', split_axis=2, concat_axis=1, tiled=True)  16.5 us
  transfers between devices with their start and end apart: 6, of which 5 were waited for; matrix products, arithmetic and copies ran while one was open for 28% of the time, Pallas kernels for 0%

profile of v1, /device:TPU:2, one launch (start us, length us, event | category | flops | bytes accessed | tf_op | source)
XLA Modules:
  0.0 669.8 jit_solution(10001107616610785118)
XLA Ops:
  9.4 12.0 %all-to-all-start.1 = ((bf16[64,2,2,256]{3,2,1,0:T(2,128)(2,1)}), bf16[64,2,2,256]{3,2,1,0:T(2,128)(2,1)S(1)}, u32[]{:S(2)}, u32[]{:S(2)}) async-start(bf16[64,2,2,256]{3,2,1,0:T(2,128)(2,1)} %stack.14), calls=%async_computation.1 | async-start | bytes 262144 | tf_op jit(solution)/shard_map/all_to_all | solution.py:73
  21.5 3.6 reduce.2
  26.0 151.7 %while.11 = (s32[]{:T(128)}, bf16[8,2,4,512]{3,1,2,0:T(2,128)(2,1)S(1)}, s32[8,15,4,512]{3,2,0,1:T(4,128)S(1)}, bf16[8,2,4,1024]{3,1,2,0:T(2,128)(2,1)S(1)}, s32[]{:T(128)}) while((s32[]{:T(128)}, bf16[8,2,4,512]{3,1,2,0:T(2,128)(2,1)S(1)}, s32[8,15,4,512]{3,2,0,1:T(4,128)S(1)}, bf16[8,2,4,1024]{3,1,2,0:T(2,128)(2,1)S(1)}, s32[]{:T(128)}) %tuple.63), condition=%wide.region_1.2_spmd, body=%wide.region_0.1_spmd.sunk | while | flops 134225920 | bytes 671825 | solution.py:54
  26.1 18.9 %fusion.123 = bf16[8,2,4,512]{3,1,2,0:T(2,128)(2,1)S(1)} fusion(bf16[8,2,4,512]{3,1,2,0:T(2,128)(2,1)S(1)} %get-tuple-element.144, s32[]{:T(128)S(6)} %copy.30, s32[4,512]{1,0:T(4,128)S(1)} %get-tuple-element.123, s32[4,512]{1,0:T(4,128)S(1)} %get-tuple-element.124, s32[4,512]{1,0:T(4,128)S(1)} %get-tuple-element.125, ...), kind=kOutput, calls=%fused_computation.85.clone.3 | convolution fusion | flops 134225920 | bytes 147460 | tf_op jit(solution)/shard_map/while/body/eval_jaxpr/cgs,gvs->cgv/dot_general | solution.py:51
  45.1 18.9 %fusion.123 = bf16[8,2,4,512]{3,1,2,0:T(2,128)(2,1)S(1)} fusion(bf16[8,2,4,512]{3,1,2,0:T(2,128)(2,1)S(1)} %get-tuple-element.144, s32[]{:T(128)S(6)} %copy.30, s32[4,512]{1,0:T(4,128)S(1)} %get-tuple-element.123, s32[4,512]{1,0:T(4,128)S(1)} %get-tuple-element.124, s32[4,512]{1,0:T(4,128)S(1)} %get-tuple-element.125, ...), kind=kOutput, calls=%fused_computation.85.clone.3 | convolution fusion | flops 134225920 | bytes 147460 | tf_op jit(solution)/shard_map/while/body/eval_jaxpr/cgs,gvs->cgv/dot_general | solution.py:51
  64.0 18.9 %fusion.123 = bf16[8,2,4,512]{3,1,2,0:T(2,128)(2,1)S(1)} fusion(bf16[8,2,4,512]{3,1,2,0:T(2,128)(2,1)S(1)} %get-tuple-element.144, s32[]{:T(128)S(6)} %copy.30, s32[4,512]{1,0:T(4,128)S(1)} %get-tuple-element.123, s32[4,512]{1,0:T(4,128)S(1)} %get-tuple-element.124, s32[4,512]{1,0:T(4,128)S(1)} %get-tuple-element.125, ...), kind=kOutput, calls=%fused_computation.85.clone.3 | convolution fusion | flops 134225920 | bytes 147460 | tf_op jit(solution)/shard_map/while/body/eval_jaxpr/cgs,gvs->cgv/dot_general | solution.py:51
  83.0 18.9 %fusion.123 = bf16[8,2,4,512]{3,1,2,0:T(2,128)(2,1)S(1)} fusion(bf16[8,2,4,512]{3,1,2,0:T(2,128)(2,1)S(1)} %get-tuple-element.144, s32[]{:T(128)S(6)} %copy.30, s32[4,512]{1,0:T(4,128)S(1)} %get-tuple-element.123, s32[4,512]{1,0:T(4,128)S(1)} %get-tuple-element.124, s32[4,512]{1,0:T(4,128)S(1)} %get-tuple-element.125, ...), kind=kOutput, calls=%fused_computation.85.clone.3 | convolution fusion | flops 134225920 | bytes 147460 | tf_op jit(solution)/shard_map/while/body/eval_jaxpr/cgs,gvs->cgv/dot_general | solution.py:51
  102.0 18.9 %fusion.123 = bf16[8,2,4,512]{3,1,2,0:T(2,128)(2,1)S(1)} fusion(bf16[8,2,4,512]{3,1,2,0:T(2,128)(2,1)S(1)} %get-tuple-element.144, s32[]{:T(128)S(6)} %copy.30, s32[4,512]{1,0:T(4,128)S(1)} %get-tuple-element.123, s32[4,512]{1,0:T(4,128)S(1)} %get-tuple-element.124, s32[4,512]{1,0:T(4,128)S(1)} %get-tuple-element.125, ...), kind=kOutput, calls=%fused_computation.85.clone.3 | convolution fusion | flops 134225920 | bytes 147460 | tf_op jit(solution)/shard_map/while/body/eval_jaxpr/cgs,gvs->cgv/dot_general | solution.py:51
  120.9 18.9 %fusion.123 = bf16[8,2,4,512]{3,1,2,0:T(2,128)(2,1)S(1)} fusion(bf16[8,2,4,512]{3,1,2,0:T(2,128)(2,1)S(1)} %get-tuple-element.144, s32[]{:T(128)S(6)} %copy.30, s32[4,512]{1,0:T(4,128)S(1)} %get-tuple-element.123, s32[4,512]{1,0:T(4,128)S(1)} %get-tuple-element.124, s32[4,512]{1,0:T(4,128)S(1)} %get-tuple-element.125, ...), kind=kOutput, calls=%fused_computation.85.clone.3 | convolution fusion | flops 134225920 | bytes 147460 | tf_op jit(solution)/shard_map/while/body/eval_jaxpr/cgs,gvs->cgv/dot_general | solution.py:51
  139.9 18.9 %fusion.123 = bf16[8,2,4,512]{3,1,2,0:T(2,128)(2,1)S(1)} fusion(bf16[8,2,4,512]{3,1,2,0:T(2,128)(2,1)S(1)} %get-tuple-element.144, s32[]{:T(128)S(6)} %copy.30, s32[4,512]{1,0:T(4,128)S(1)} %get-tuple-element.123, s32[4,512]{1,0:T(4,128)S(1)} %get-tuple-element.124, s32[4,512]{1,0:T(4,128)S(1)} %get-tuple-element.125, ...), kind=kOutput, calls=%fused_computation.85.clone.3 | convolution fusion | flops 134225920 | bytes 147460 | tf_op jit(solution)/shard_map/while/body/eval_jaxpr/cgs,gvs->cgv/dot_general | solution.py:51
  158.9 18.9 %fusion.123 = bf16[8,2,4,512]{3,1,2,0:T(2,128)(2,1)S(1)} fusion(bf16[8,2,4,512]{3,1,2,0:T(2,128)(2,1)S(1)} %get-tuple-element.144, s32[]{:T(128)S(6)} %copy.30, s32[4,512]{1,0:T(4,128)S(1)} %get-tuple-element.123, s32[4,512]{1,0:T(4,128)S(1)} %get-tuple-element.124, s32[4,512]{1,0:T(4,128)S(1)} %get-tuple-element.125, ...), kind=kOutput, calls=%fused_computation.85.clone.3 | convolution fusion | flops 134225920 | bytes 147460 | tf_op jit(solution)/shard_map/while/body/eval_jaxpr/cgs,gvs->cgv/dot_general | solution.py:51
  178.0 12.9 %copy.17 = bf16[2,2,16384]{1,0,2:T(2,128)(2,1)} copy(bf16[2,2,16384]{2,1,0:T(2,128)(2,1)S(1)} %pad_maximum_fusion.2) | data formatting | bytes 262144 | tf_op jit(solution)/shard_map/stack | solution.py:69
  190.9 13.7 %reshape.637 = bf16[64,2,512]{2,1,0:T(2,128)(2,1)} reshape(bf16[16384,2,2]{2,1,0:T(2,128)(2,1)} %bitcast.150) | data formatting | bytes 262144
  204.7 10.3 %all-to-all-start = ((bf16[64,2,512]{2,1,0:T(2,128)(2,1)}), bf16[64,2,512]{2,1,0:T(2,128)(2,1)S(1)}, u32[]{:S(2)}, u32[]{:S(2)}) async-start(bf16[64,2,512]{2,1,0:T(2,128)(2,1)} %reshape.637), calls=%async_computation | async-start | bytes 262144 | tf_op jit(solution)/shard_map/all_to_all | solution.py:19
  215.4 9.0 %all-to-all-done = bf16[64,2,512]{2,1,0:T(2,128)(2,1)S(1)} async-done(((bf16[64,2,512]{2,1,0:T(2,128)(2,1)}), bf16[64,2,512]{2,1,0:T(2,128)(2,1)S(1)}, u32[]{:S(2)}, u32[]{:S(2)}) %all-to-all-start) | async-done | bytes 131104 | tf_op jit(solution)/shard_map/all_to_all | solution.py:19
  224.4 19.0 %reshape.638 = bf16[16384,2,2]{2,1,0:T(2,128)(2,1)} reshape(bf16[64,2,512]{2,1,0:T(2,128)(2,1)S(1)} %all-to-all-done) | data formatting | bytes 262144
  243.4 16.5 %copy.18 = bf16[2,2,64,256]{3,0,1,2:T(2,128)(2,1)S(1)} copy(bf16[2,2,64,256]{1,0,3,2:T(2,128)(2,1)} %bitcast.151) | data formatting | bytes 262144 | tf_op jit(solution)/shard_map/all_to_all | solution.py:19
  260.9 7.5 %gather_fusion = bf16[2048,256]{1,0:T(8,128)(2,1)S(1)} fusion(bf16[256,256]{1,0:T(8,128)(2,1)S(1)} %get-tuple-element.81, s32[2048]{0:T(1024)S(1)} %broadcast_clamp_fusion), kind=kCustom, calls=%fused_computation | custom fusion | bytes 2105344 | tf_op jit(solution)/shard_map/gather | solution.py:82
  269.6 6.0 all-to-all-start.2
  276.0 26.6 %all-to-all-done.2 = bf16[64,32,256]{2,1,0:T(8,128)(2,1)S(1)} async-done(((bf16[64,32,256]{2,1,0:T(8,128)(2,1)}), bf16[64,32,256]{2,1,0:T(8,128)(2,1)S(1)}, u32[]{:S(2)}, u32[]{:S(2)}) %all-to-all-start.2) | async-done | bytes 1048608 | tf_op jit(solution)/shard_map/all_to_all | solution.py:84
  319.0 2.8 scatter_fusion
  321.9 2.8 scatter_fusion.1
  324.7 3.0 scatter_fusion.2
  327.7 2.8 scatter_fusion.3
  330.5 2.8 scatter_fusion.4
  345.8 8.0 %all-to-all-start.3 = ((bf16[64,32,256]{2,1,0:T(8,128)(2,1)}), bf16[64,32,256]{2,1,0:T(8,128)(2,1)}, u32[]{:S(2)}, u32[]{:S(2)}) async-start(bf16[64,32,256]{2,1,0:T(8,128)(2,1)} %bitcast.58), calls=%async_computation.3 | async-start | bytes 2097152 | tf_op jit(solution)/shard_map/all_to_all | solution.py:121
  354.1 26.6 %all-to-all-done.3 = bf16[64,32,256]{2,1,0:T(8,128)(2,1)} async-done(((bf16[64,32,256]{2,1,0:T(8,128)(2,1)}), bf16[64,32,256]{2,1,0:T(8,128)(2,1)}, u32[]{:S(2)}, u32[]{:S(2)}) %all-to-all-start.3) | async-done | bytes 1048608 | tf_op jit(solution)/shard_map/all_to_all | solution.py:121
  382.2 11.9 %scatter_fusion.9 = f32[256,256]{1,0:T(8,128)S(1)} fusion(f32[256,256]{1,0:T(8,128)S(1)} %convolution_add_fusion, s32[2048]{0:T(1024)S(1)} %reshape.456, f32[2048,256]{1,0:T(8,128)S(1)} %bitcast.152), kind=kCustom, calls=%fused_computation.21 | custom fusion | flops 524288 | bytes 6299648 | tf_op jit(solution)/shard_map/scatter-add | solution.py:129
  396.2 79.4 %all-gather.2.cloned.1.call-done = bf16[16384,256]{1,0:T(8,128)(2,1)} async-done(((bf16[256,256]{1,0:T(8,128)(2,1)}), bf16[16384,256]{1,0:T(8,128)(2,1)}) %all-gather.2.cloned.1.call-update) | async-done | bytes 8388624 | tf_op jit(solution)/shard_map/all_gather | solution.py:134
  475.7 4.7 fusion.75
  480.4 11.1 %psum.14 = f32[2,2,256]{2,1,0:T(2,128)} all-reduce(f32[2,2,256]{2,1,0:T(2,128)S(1)} %fusion.75), channel_id=1, replica_groups=mesh['feat'=64,'rep'=4] {'rep'}, use_global_device_ids=true, to_apply=%region_13.14 | all-reduce | flops 1024 | bytes 8192 | tf_op jit(solution)/shard_map/psum | solution.py:137
  491.5 168.8 %all-reduce.2.cloned.1.call-done = f32[2,256,256]{2,1,0:T(8,128)} async-done(((f32[2,256,256]{2,1,0:T(8,128)}), f32[2,256,256]{2,1,0:T(8,128)}) %all-reduce.2.cloned.1.call-update) | async-done | bytes 524304 | tf_op jit(solution)/shard_map/psum | solution.py:109
  (96 shorter events, 40.5 us)
Async XLA Ops:
  8.0 18.0 %copy-start.2 = (bf16[1,2,32768]{2,1,0:T(2,128)(2,1)S(1)}, bf16[1,2,32768]{2,1,0:T(2,128)(2,1)}, u32[]{:S(2)}) copy-start(bf16[1,2,32768]{2,1,0:T(2,128)(2,1)} %param.12) | copy-start | bytes 393220
  9.4 195.2 %all-to-all-start.1 = ((bf16[64,2,2,256]{3,2,1,0:T(2,128)(2,1)}), bf16[64,2,2,256]{3,2,1,0:T(2,128)(2,1)S(1)}, u32[]{:S(2)}, u32[]{:S(2)}) async-start(bf16[64,2,2,256]{3,2,1,0:T(2,128)(2,1)} %stack.14), calls=%async_computation.1 | async-start | bytes 262144 | tf_op jit(solution)/shard_map/all_to_all | solution.py:73
  190.9 13.7 %copy-start.3 = (s32[1,1,64,32]{2,3,1,0:T(8,128)S(1)}, s32[1,1,64,32]{2,3,1,0:T(8,128)}, u32[]{:S(2)}) copy-start(s32[1,1,64,32]{2,3,1,0:T(8,128)} %param.16) | copy-start | bytes 24580
  190.9 24.1 %copy-start.5 = (s32[1,1,64]{2,1,0:T(1,128)S(1)}, s32[1,1,64]{2,1,0:T(1,128)}, u32[]{:S(2)}) copy-start(s32[1,1,64]{2,1,0:T(1,128)} %param.17) | copy-start | bytes 772
  204.7 19.7 %all-to-all-start = ((bf16[64,2,512]{2,1,0:T(2,128)(2,1)}), bf16[64,2,512]{2,1,0:T(2,128)(2,1)S(1)}, u32[]{:S(2)}, u32[]{:S(2)}) async-start(bf16[64,2,512]{2,1,0:T(2,128)(2,1)} %reshape.637), calls=%async_computation | async-start | bytes 262144 | tf_op jit(solution)/shard_map/all_to_all | solution.py:19
  268.4 7.3 %copy-start.4 = (s32[1,10,256]{2,0,1:T(1,128)S(1)}, s32[1,10,256]{2,0,1:T(1,128)}, u32[]{:S(2)}) copy-start(s32[1,10,256]{2,0,1:T(1,128)} %param.18) | copy-start | bytes 30724
  268.4 7.4 %copy-start = (bf16[2,256,256]{2,1,0:T(8,128)(2,1)S(1)}, bf16[2,256,256]{2,1,0:T(8,128)(2,1)}, u32[]{:S(2)}) copy-start(bf16[2,256,256]{2,1,0:T(8,128)(2,1)} %param.15) | copy-start | bytes 786436
  269.6 33.0 %all-to-all-start.2 = ((bf16[64,32,256]{2,1,0:T(8,128)(2,1)}), bf16[64,32,256]{2,1,0:T(8,128)(2,1)S(1)}, u32[]{:S(2)}, u32[]{:S(2)}) async-start(bf16[64,32,256]{2,1,0:T(8,128)(2,1)} %broadcast_select_fusion), calls=%async_computation.2 | async-start | bytes 2097152 | tf_op jit(solution)/shard_map/all_to_all | solution.py:84
  345.8 34.8 %all-to-all-start.3 = ((bf16[64,32,256]{2,1,0:T(8,128)(2,1)}), bf16[64,32,256]{2,1,0:T(8,128)(2,1)}, u32[]{:S(2)}, u32[]{:S(2)}) async-start(bf16[64,32,256]{2,1,0:T(8,128)(2,1)} %bitcast.58), calls=%async_computation.3 | async-start | bytes 2097152 | tf_op jit(solution)/shard_map/all_to_all | solution.py:121
  353.8 121.9 %all-gather.2.cloned.1.call-start = ((), (), s32[]{:S(2)}) async-start(), calls=%async_computation.4 | async-start | bytes 8519680 | tf_op jit(solution)/shard_map/all_gather | solution.py:134
  382.2 11.9 %copy-start.1 = (f32[256,256]{1,0:T(8,128)S(1)}, f32[256,256]{1,0:T(8,128)}, u32[]{:S(2)}) copy-start(f32[256,256]{1,0:T(8,128)} %get-tuple-element.82) | copy-start | bytes 786436
  394.9 265.4 %all-reduce.2.cloned.1.call-start = ((), (), s32[]{:S(2)}) async-start(), calls=%async_computation.5 | async-start | bytes 1048576 | tf_op jit(solution)/shard_map/psum | solution.py:109
Sparse Core Ops, SparseCore 0:
  395.0 80.6 all-gather.1
Sparse Core Ops, SparseCore 1:
  401.4 258.8 all-reduce.1
